TPU v7x, 32 devices: a whole 2x2x4 slice. The times are simulated.
32 devices in a mesh: ctx: 16 (over z, y, x), head: 2 (over core).
Axes of the slice: x: 2, y: 2, z: 4, core: 2. Of those that a mesh axis runs over, the one named last changes fastest.
Arguments:
- activations: bfloat16 [7168, 4096], P('ctx'), may hold values from -150 to 150
- query_weight: bfloat16 [4096, 2048], P('ctx', 'head'), may hold values from -0.09375 to 0.09375
- keyval_weight: bfloat16 [4096, 2, 2048], P('ctx', None, 'head'), may hold values from -0.09375 to 0.09375
- out_weight: bfloat16 [2048, 4096], P('head', 'ctx'), may hold values from -0.125 to 0.125
- norm_gain: float32 [4096], replicated, may hold values from 0.1 to 1.9
- vocab_weight: bfloat16 [63488, 4096], P(('ctx', 'head')), may hold values from -15 to 15
- mask_positions: int32 [16, 16], P('ctx'), may hold values from 0 to 447, as said below
- mask_count: int32 [16], P('ctx'), may hold values from 1 to 16, as said below
- targets: int32 [16, 16], P('ctx'), may hold values from 0 to 63487
Outputs:
- loss: float32 [16, 16], P('ctx')
Inputs may be any that keep to these rules, and one draw needn't show every extreme that they name: `mask_positions`: the 16 entries of a row are distinct; the first mask_count[c] of row c are the masked positions of block c, the others unused. `mask_count`: some block has all 16 slots used.
All inputs are finite; a program needn't handle non-finite values.
Results may differ from a plain program's by a relative error of at most 0.0098.
Values may be sent and summed in bfloat16 or wider, within the bound.
No kernel may reach another device: no remote copies, remote signals or barrier semaphores. Data moves between devices by JAX's collectives and lax.ppermute only.
A program may use at most 128 MiB of HBM per device.

v0:
```python
import jax
import jax.numpy as jnp
from jax import lax
from jax.sharding import PartitionSpec as P

HDIM = 128


def shards(
    activations,
    query_weight,
    keyval_weight,
    out_weight,
    norm_gain,
    vocab_weight,
    mask_positions,
    mask_count,
    targets,
):
    ctx_count = lax.axis_size("ctx")
    block_len = activations.shape[0]
    slot_count = mask_positions.shape[1]
    total_rows = ctx_count * slot_count
    head_columns = query_weight.shape[1]
    heads_here = head_columns // HDIM
    feature_cols = activations
    keyval = jnp.einsum(
        "td,djc->tjc",
        feature_cols,
        lax.all_gather(keyval_weight, "ctx", axis=0, tiled=True),
        preferred_element_type=jnp.float32,
    ).astype(jnp.bfloat16)
    key_heads = keyval[:, 0].reshape(block_len, heads_here, HDIM)
    value_heads = keyval[:, 1].reshape(block_len, heads_here, HDIM)
    rows_here = jnp.take(activations, mask_positions[0], axis=0)
    feature_cols = rows_here
    own_queries = jnp.dot(
        feature_cols,
        lax.all_gather(query_weight, "ctx", axis=0, tiled=True),
        preferred_element_type=jnp.float32,
    ).astype(jnp.bfloat16)
    queries = lax.all_gather(own_queries, "ctx", axis=0, tiled=True)
    query_heads = queries.reshape(total_rows, heads_here, HDIM)
    scores = jnp.einsum(
        "rhc,thc->hrt", query_heads, key_heads, preferred_element_type=jnp.float32
    ) * HDIM ** (-0.5)
    highest = lax.pmax(jnp.max(scores, axis=2), "ctx")
    exponent = jnp.exp(scores - highest[:, :, None])
    weights = exponent.astype(jnp.bfloat16)
    numerator = jnp.einsum(
        "hrt,thc->rhc", weights, value_heads, preferred_element_type=jnp.float32
    ).reshape(total_rows, head_columns)
    denominator = jnp.sum(exponent, axis=2).T
    numerator, denominator = (
        lax.psum_scatter(numerator, "ctx", scatter_dimension=0, tiled=True),
        lax.psum_scatter(denominator, "ctx", scatter_dimension=0, tiled=True),
    )
    attended = (
        (numerator.reshape(slot_count, heads_here, HDIM) / denominator[:, :, None])
        .reshape(slot_count, head_columns)
        .astype(jnp.bfloat16)
    )
    branch_part = jnp.dot(
        attended,
        lax.all_gather(out_weight, "ctx", axis=1, tiled=True),
        preferred_element_type=jnp.float32,
    )
    wanted = lax.all_gather(targets, "ctx", axis=0, tiled=True)
    branch = lax.psum_scatter(branch_part, "head", scatter_dimension=0, tiled=True)
    meansquare = jnp.mean(branch * branch, axis=1, keepdims=True)
    hidden = (branch * lax.rsqrt(meansquare + 1e-06) * norm_gain).astype(jnp.bfloat16)
    gathered = lax.all_gather(hidden, ("ctx", "head"), axis=0, tiled=True)
    logits = lax.dot_general(
        gathered, vocab_weight, (((1,), (1,)), ((), ())), preferred_element_type=jnp.float32
    )
    vocab_start = lax.axis_index(("ctx", "head")) * vocab_weight.shape[0]
    vocab_ids = vocab_start + jnp.arange(vocab_weight.shape[0], dtype=jnp.int32)
    wanted_rows = wanted.reshape(total_rows)
    largest = lax.pmax(jnp.max(logits, axis=1), ("ctx", "head"))
    expsum = jnp.sum(jnp.exp(logits - largest[:, None]), axis=1)
    picked = jnp.sum(jnp.where(vocab_ids[None, :] == wanted_rows[:, None], logits, 0.0), axis=1)
    expsum, picked = lax.psum((expsum, picked), ("ctx", "head"))
    losses = (largest + jnp.log(expsum) - picked).reshape(ctx_count, slot_count)
    block_losses = lax.dynamic_slice_in_dim(losses, lax.axis_index("ctx"), 1, 0)[0]
    active = jnp.arange(slot_count, dtype=jnp.int32) < mask_count[0]
    return jnp.where(active, block_losses, jnp.zeros_like(block_losses))[None, :]


def solution(mesh):
    in_specs = (
        P("ctx", None),
        P("ctx", "head"),
        P("ctx", None, "head"),
        P("head", "ctx"),
        P(),
        P(("ctx", "head"), None),
        P("ctx", None),
        P("ctx"),
        P("ctx", None),
    )
    out_specs = P("ctx", None)
    return jax.shard_map(shards, mesh=mesh, in_specs=in_specs, out_specs=out_specs, check_vma=False)
```

profile of v0, /device:TPU:0, one launch (start us, length us, event | category | flops | bytes accessed | tf_op | source)
XLA Modules:
  0.0 831.2 jit_solution(3566141470585280756)
XLA Ops:
  7.3 2.6 copy.14
  10.0 3.3 gather_fusion
  13.3 112.4 %all-gather.8.cloned.1.call-done = bf16[4096,1024]{1,0:T(8,128)(2,1)} async-done(((bf16[256,1024]{1,0:T(8,128)(2,1)}), bf16[4096,1024]{1,0:T(8,128)(2,1)}) %all-gather.8.cloned.1.call-update) | async-done | bytes 8388624 | tf_op jit(solution)/shard_map/all_gather | solution.py:39
  125.7 4.6 convolution_convert_fusion
  130.3 44.7 %all_gather.20 = bf16[256,1024]{1,0:T(8,128)(2,1)S(1)} all-gather(bf16[16,1024]{1,0:T(8,128)(2,1)S(1)} %convolution_convert_fusion), channel_id=1, replica_groups=mesh['ctx'=16,'head'=2] {'ctx'}, dimensions={0}, use_global_device_ids=true | all-gather | bytes 557056 | tf_op jit(solution)/shard_map/all_gather | solution.py:42
  175.0 147.0 %all-gather.6.cloned.1.call-done = bf16[4096,2,1024]{2,0,1:T(8,128)(2,1)} async-done(((bf16[256,2,1024]{2,0,1:T(8,128)(2,1)}), bf16[4096,2,1024]{2,0,1:T(8,128)(2,1)}) %all-gather.6.cloned.1.call-update) | async-done | bytes 16777232 | tf_op jit(solution)/shard_map/all_gather | solution.py:30
  322.0 12.6 %fusion.8 = bf16[448,2,1024]{2,0,1:T(8,128)(2,1)S(1)} fusion(bf16[4096,2,1024]{2,0,1:T(8,128)(2,1)} %all-gather.6.cloned.1.call-done, bf16[448,4096]{1,0:T(8,128)(2,1)} %param.9), kind=kOutput, calls=%fused_computation.12 | convolution fusion | flops 7517110272 | bytes 22282240 | tf_op jit(solution)/shard_map/td,djc->tjc/dot_general | solution.py:27
  334.9 2.4 multiply_reduce_fusion
  337.4 39.4 %pmax.14 = f32[8,256]{1,0:T(8,128)S(1)} all-reduce(f32[8,256]{1,0:T(8,128)S(1)} %get-tuple-element.11), channel_id=1, replica_groups=mesh['ctx'=16,'head'=2] {'ctx'}, use_global_device_ids=true, to_apply=%region_1.2 | all-reduce | flops 2048 | bytes 16384 | tf_op jit(solution)/shard_map/pmax | solution.py:47
  376.9 2.7 fusion.2
  380.5 2.9 fusion.4
  383.4 1.4 copy.18
  385.4 66.8 %reduce-scatter.12.cloned.1.call-done = f32[16,8]{1,0:T(8,128)} async-done(((f32[256,8]{1,0:T(8,128)}), f32[16,8]{1,0:T(8,128)}) %reduce-scatter.12.cloned.1.call-update) | async-done | bytes 528
  453.0 75.5 %reduce-scatter.10.cloned.1.call-done = f32[16,1024]{1,0:T(8,128)} async-done(((f32[256,1024]{1,0:T(8,128)}), f32[16,1024]{1,0:T(8,128)}) %reduce-scatter.10.cloned.1.call-update) | async-done | bytes 65552
  529.6 133.2 %all-gather.10.cloned.1.call-done = bf16[1024,4096]{1,0:T(8,128)(2,1)} async-done(((bf16[1024,256]{1,0:T(8,128)(2,1)}), bf16[1024,4096]{1,0:T(8,128)(2,1)}) %all-gather.10.cloned.1.call-update) | async-done | bytes 8388624 | tf_op jit(solution)/shard_map/all_gather | solution.py:65
  662.8 5.3 fusion.24
  668.2 6.0 reduce-scatter.8.cloned.1.call-done
  674.2 1.0 multiply_reduce_fusion.1
  675.2 1.6 multiply_convert_fusion
  676.9 40.8 %all-gather = s32[16,1,16]{2,1,0:T(1,128)S(1)} all-gather(s32[1,1,16]{2,1,0:T(1,128)S(1)} %bitcast.53), channel_id=1, replica_groups=mesh['ctx'=16,'head'=2] {'ctx'}, dimensions={0}, use_global_device_ids=true | all-gather | bytes 1088 | tf_op jit(solution)/shard_map/all_gather | solution.py:68
  719.6 15.4 %all-gather.12.cloned.1.call-done = bf16[256,4096]{1,0:T(8,128)(2,1)} async-done(((bf16[8,4096]{1,0:T(8,128)(2,1)}), bf16[256,4096]{1,0:T(8,128)(2,1)}) %all-gather.12.cloned.1.call-update) | async-done | bytes 2097168 | tf_op jit(solution)/shard_map/all_gather | solution.py:72
  735.0 8.6 %fusion.23 = (f32[256]{0:T(256)S(1)}, f32[256,1984]{0,1:T(8,128)S(1)}) fusion(bf16[256,4096]{1,0:T(8,128)(2,1)} %all-gather.12.cloned.1.call-done, bf16[1984,4096]{1,0:T(8,128)(2,1)} %param.14), kind=kOutput, calls=%fused_computation.39 | convolution fusion | flops 4161257216 | bytes 20382720 | tf_op jit(solution)/shard_map/dot_general | solution.py:73
  743.6 38.7 %pmax.15 = f32[256]{0:T(256)S(1)} all-reduce(f32[256]{0:T(256)S(1)} %get-tuple-element.13), channel_id=1, replica_groups=mesh['ctx'=16,'head'=2] {'ctx','head'}, use_global_device_ids=true, to_apply=%region_8.9 | all-reduce | flops 256 | bytes 2048 | tf_op jit(solution)/shard_map/pmax | solution.py:79
  783.2 40.5 %all-reduce = (f32[256]{0:T(256)S(1)}, f32[256]{0:T(256)S(1)}) all-reduce(f32[256]{0:T(256)S(1)} %get-tuple-element.6, f32[256]{0:T(256)S(1)} %get-tuple-element.5), channel_id=1, replica_groups=mesh['ctx'=16,'head'=2] {'ctx','head'}, use_global_device_ids=true, to_apply=%region_12.13 | all-reduce | flops 512 | bytes 4096 | tf_op jit(solution)/shard_map/psum | solution.py:82
  (39 shorter events, 7.7 us)
Async XLA Ops:
  6.5 3.4 copy-start.2
  6.5 119.2 %all-gather.8.cloned.1.call-start = ((), (), s32[]{:S(2)}) async-start(), calls=%async_computation.4 | async-start | bytes 8912896 | tf_op jit(solution)/shard_map/all_gather | solution.py:39
  7.3 314.7 %all-gather.6.cloned.1.call-start = ((), (), s32[]{:S(2)}) async-start(), calls=%async_computation.3 | async-start | bytes 17825792 | tf_op jit(solution)/shard_map/all_gather | solution.py:30
  9.9 442.4 %reduce-scatter.12.cloned.1.call-start = ((), (), s32[]{:S(2)}) async-start(), calls=%async_computation.9 | async-start | bytes 139264
  380.4 148.1 %reduce-scatter.10.cloned.1.call-start = ((), (), s32[]{:S(2)}) async-start(), calls=%async_computation.8 | async-start | bytes 1114112
  384.8 278.0 %all-gather.10.cloned.1.call-start = ((), (), s32[]{:S(2)}) async-start(), calls=%async_computation.5 | async-start | bytes 8912896 | tf_op jit(solution)/shard_map/all_gather | solution.py:65
  385.4 288.8 %reduce-scatter.8.cloned.1.call-start = ((), (), s32[]{:S(2)}) async-start(), calls=%async_computation.6 | async-start | bytes 393216 | tf_op jit(solution)/shard_map/reduce_scatter | solution.py:69
  529.6 145.6 %copy-start = (f32[4096]{0:T(1024)S(1)}, f32[4096]{0:T(1024)}, u32[]{:S(2)}) copy-start(f32[4096]{0:T(1024)} %param.13) | copy-start | bytes 49156
  529.6 147.3 %copy-start.1 = (s32[1,16]{1,0:T(1,128)S(1)}, s32[1,16]{1,0:T(1,128)}, u32[]{:S(2)}) copy-start(s32[1,16]{1,0:T(1,128)} %param.17) | copy-start | bytes 196
  668.2 66.9 %all-gather.12.cloned.1.call-start = ((), (), s32[]{:S(2)}) async-start(), calls=%async_computation.7 | async-start | bytes 2162688 | tf_op jit(solution)/shard_map/all_gather | solution.py:72
Sparse Core Ops, SparseCore 0:
  10.1 115.5 all-gather.7
  128.5 193.4 all-gather.5
  380.5 71.6 reduce-scatter.11
  454.5 74.0 reduce-scatter.9
  531.1 131.7 all-gather.9
  668.3 5.8 reduce-scatter.7
  677.4 57.5 all-gather.11
where the time goes:
time: 832 us; the launch traced here: 831 us
  waiting for transfers between devices  558 us (67%)
  blocking collectives  204 us (25%)
  matrix products  36.4 us (4%)
  between operations  14.3 us (2%)
  local copies, waits for them, and re-layouts  11.1 us (1%)
    all_gather x1, waiting for transfers between devices, shards(): lax.all_gather(keyval_weight, 'ctx', axis=0, tiled=True)  147 us
    unnamed x9, waiting for transfers between devices  144 us
    all_gather x1, waiting for transfers between devices, shards(): lax.all_gather(out_weight, 'ctx', axis=1, tiled=True)  133 us
    all_gather x1, waiting for transfers between devices, shards(): lax.all_gather(query_weight, 'ctx', axis=0, tiled=True)  112 us
    all_gather x1, blocking collectives, shards(): queries = lax.all_gather(own_queries, 'ctx', axis=0, tiled=True)  44.7 us
    all_gather x1, blocking collectives, shards(): wanted = lax.all_gather(targets, 'ctx', axis=0, tiled=True)  40.8 us
    psum x1, blocking collectives, shards(): expsum, picked = lax.psum((expsum, picked), ('ctx', 'head'))  40.5 us
    pmax x1, blocking collectives, shards(): highest = lax.pmax(jnp.max(scores, axis=2), 'ctx')  39.4 us
  transfers between devices with their start and end apart: 7, of which 7 were waited for; matrix products, arithmetic and copies ran while one was open for 2% of the time, Pallas kernels for 0%

commit v1 on v0

--- a/solution.py
+++ b/solution.py
@@ -79,7 +79,7 @@
     largest = lax.pmax(jnp.max(logits, axis=1), ("ctx", "head"))
     expsum = jnp.sum(jnp.exp(logits - largest[:, None]), axis=1)
     picked = jnp.sum(jnp.where(vocab_ids[None, :] == wanted_rows[:, None], logits, 0.0), axis=1)
-    expsum, picked = lax.psum((expsum, picked), ("ctx", "head"))
+    expsum, picked = lax.psum(lax.psum((expsum, picked), "head"), "ctx")
     losses = (largest + jnp.log(expsum) - picked).reshape(ctx_count, slot_count)
     block_losses = lax.dynamic_slice_in_dim(losses, lax.axis_index("ctx"), 1, 0)[0]
     active = jnp.arange(slot_count, dtype=jnp.int32) < mask_count[0]

time: 832 us -> 834 us (level)
    psum x1 -> x2, blocking collectives: 40.5 us -> 43 us  [shards(): expsum, picked = lax.psum(lax.psum((expsum, picked), 'head'), 'ctx')]
where the time goes in v1:
time: 834 us
  waiting for transfers between devices  558 us (67%)
  blocking collectives  207 us (25%)
  matrix products  36.4 us (4%)
  between operations  14.3 us (2%)
  local copies, waits for them, and re-layouts  11.1 us (1%)
    all_gather x1, waiting for transfers between devices, shards(): lax.all_gather(keyval_weight, 'ctx', axis=0, tiled=True)  147 us
    unnamed x9, waiting for transfers between devices  144 us
    all_gather x1, waiting for transfers between devices, shards(): lax.all_gather(out_weight, 'ctx', axis=1, tiled=True)  133 us
    all_gather x1, waiting for transfers between devices, shards(): lax.all_gather(query_weight, 'ctx', axis=0, tiled=True)  112 us
    all_gather x1, blocking collectives, shards(): queries = lax.all_gather(own_queries, 'ctx', axis=0, tiled=True)  44.7 us
    psum x2, blocking collectives, shards(): expsum, picked = lax.psum(lax.psum((expsum, picked), 'head'), 'ctx')  43 us
    all_gather x1, blocking collectives, shards(): wanted = lax.all_gather(targets, 'ctx', axis=0, tiled=True)  40.8 us
    pmax x1, blocking collectives, shards(): highest = lax.pmax(jnp.max(scores, axis=2), 'ctx')  39.4 us
  transfers between devices with their start and end apart: 7, of which 7 were waited for; matrix products, arithmetic and copies ran while one was open for 2% of the time, Pallas kernels for 0%

profile of v1, /device:TPU:0, one launch (start us, length us, event | category | flops | bytes accessed | tf_op | source)
XLA Modules:
  0.0 833.7 jit_solution(2480603452913706395)
XLA Ops:
  7.3 2.6 copy.14
  10.0 3.3 gather_fusion
  13.3 112.4 %all-gather.8.cloned.1.call-done = bf16[4096,1024]{1,0:T(8,128)(2,1)} async-done(((bf16[256,1024]{1,0:T(8,128)(2,1)}), bf16[4096,1024]{1,0:T(8,128)(2,1)}) %all-gather.8.cloned.1.call-update) | async-done | bytes 8388624 | tf_op jit(solution)/shard_map/all_gather | solution.py:39
  125.7 4.6 convolution_convert_fusion
  130.3 44.7 %all_gather.20 = bf16[256,1024]{1,0:T(8,128)(2,1)S(1)} all-gather(bf16[16,1024]{1,0:T(8,128)(2,1)S(1)} %convolution_convert_fusion), channel_id=1, replica_groups=mesh['ctx'=16,'head'=2] {'ctx'}, dimensions={0}, use_global_device_ids=true | all-gather | bytes 557056 | tf_op jit(solution)/shard_map/all_gather | solution.py:42
  175.0 147.0 %all-gather.6.cloned.1.call-done = bf16[4096,2,1024]{2,0,1:T(8,128)(2,1)} async-done(((bf16[256,2,1024]{2,0,1:T(8,128)(2,1)}), bf16[4096,2,1024]{2,0,1:T(8,128)(2,1)}) %all-gather.6.cloned.1.call-update) | async-done | bytes 16777232 | tf_op jit(solution)/shard_map/all_gather | solution.py:30
  322.0 12.6 %fusion.8 = bf16[448,2,1024]{2,0,1:T(8,128)(2,1)S(1)} fusion(bf16[4096,2,1024]{2,0,1:T(8,128)(2,1)} %all-gather.6.cloned.1.call-done, bf16[448,4096]{1,0:T(8,128)(2,1)} %param.9), kind=kOutput, calls=%fused_computation.12 | convolution fusion | flops 7517110272 | bytes 22282240 | tf_op jit(solution)/shard_map/td,djc->tjc/dot_general | solution.py:27
  334.9 2.4 multiply_reduce_fusion
  337.4 39.4 %pmax.14 = f32[8,256]{1,0:T(8,128)S(1)} all-reduce(f32[8,256]{1,0:T(8,128)S(1)} %get-tuple-element.13), channel_id=1, replica_groups=mesh['ctx'=16,'head'=2] {'ctx'}, use_global_device_ids=true, to_apply=%region_1.2 | all-reduce | flops 2048 | bytes 16384 | tf_op jit(solution)/shard_map/pmax | solution.py:47
  376.9 2.7 fusion.2
  380.5 2.9 fusion.4
  383.4 1.4 copy.18
  385.4 66.8 %reduce-scatter.12.cloned.1.call-done = f32[16,8]{1,0:T(8,128)} async-done(((f32[256,8]{1,0:T(8,128)}), f32[16,8]{1,0:T(8,128)}) %reduce-scatter.12.cloned.1.call-update) | async-done | bytes 528
  453.0 75.5 %reduce-scatter.10.cloned.1.call-done = f32[16,1024]{1,0:T(8,128)} async-done(((f32[256,1024]{1,0:T(8,128)}), f32[16,1024]{1,0:T(8,128)}) %reduce-scatter.10.cloned.1.call-update) | async-done | bytes 65552
  529.6 133.2 %all-gather.10.cloned.1.call-done = bf16[1024,4096]{1,0:T(8,128)(2,1)} async-done(((bf16[1024,256]{1,0:T(8,128)(2,1)}), bf16[1024,4096]{1,0:T(8,128)(2,1)}) %all-gather.10.cloned.1.call-update) | async-done | bytes 8388624 | tf_op jit(solution)/shard_map/all_gather | solution.py:65
  662.8 5.3 fusion.24
  668.2 6.0 reduce-scatter.8.cloned.1.call-done
  675.2 1.6 multiply_convert_fusion
  676.9 40.8 %all-gather = s32[16,1,16]{2,1,0:T(1,128)S(1)} all-gather(s32[1,1,16]{2,1,0:T(1,128)S(1)} %bitcast.53), channel_id=1, replica_groups=mesh['ctx'=16,'head'=2] {'ctx'}, dimensions={0}, use_global_device_ids=true | all-gather | bytes 1088 | tf_op jit(solution)/shard_map/all_gather | solution.py:68
  719.6 15.4 %all-gather.12.cloned.1.call-done = bf16[256,4096]{1,0:T(8,128)(2,1)} async-done(((bf16[8,4096]{1,0:T(8,128)(2,1)}), bf16[256,4096]{1,0:T(8,128)(2,1)}) %all-gather.12.cloned.1.call-update) | async-done | bytes 2097168 | tf_op jit(solution)/shard_map/all_gather | solution.py:72
  735.0 8.6 %fusion.23 = (f32[256]{0:T(256)S(1)}, f32[256,1984]{0,1:T(8,128)S(1)}) fusion(bf16[256,4096]{1,0:T(8,128)(2,1)} %all-gather.12.cloned.1.call-done, bf16[1984,4096]{1,0:T(8,128)(2,1)} %param.14), kind=kOutput, calls=%fused_computation.39 | convolution fusion | flops 4161257216 | bytes 20382720 | tf_op jit(solution)/shard_map/dot_general | solution.py:73
  743.6 38.7 %pmax.15 = f32[256]{0:T(256)S(1)} all-reduce(f32[256]{0:T(256)S(1)} %get-tuple-element.15), channel_id=1, replica_groups=mesh['ctx'=16,'head'=2] {'ctx','head'}, use_global_device_ids=true, to_apply=%region_8.9 | all-reduce | flops 256 | bytes 2048 | tf_op jit(solution)/shard_map/pmax | solution.py:79
  783.2 2.5 all-reduce.1
  785.7 40.5 %all-reduce = (f32[256]{0:T(256)S(1)}, f32[256]{0:T(256)S(1)}) all-reduce(f32[256]{0:T(256)S(1)} %get-tuple-element.9, f32[256]{0:T(256)S(1)} %get-tuple-element.10), channel_id=1, replica_groups=mesh['ctx'=16,'head'=2] {'ctx'}, use_global_device_ids=true, to_apply=%region_14.15 | all-reduce | flops 512 | bytes 4096 | tf_op jit(solution)/shard_map/psum | solution.py:82
  (40 shorter events, 8.7 us)
Async XLA Ops:
  6.5 3.4 copy-start.2
  6.5 119.2 %all-gather.8.cloned.1.call-start = ((), (), s32[]{:S(2)}) async-start(), calls=%async_computation.4 | async-start | bytes 8912896 | tf_op jit(solution)/shard_map/all_gather | solution.py:39
  7.3 314.7 %all-gather.6.cloned.1.call-start = ((), (), s32[]{:S(2)}) async-start(), calls=%async_computation.3 | async-start | bytes 17825792 | tf_op jit(solution)/shard_map/all_gather | solution.py:30
  9.9 442.4 %reduce-scatter.12.cloned.1.call-start = ((), (), s32[]{:S(2)}) async-start(), calls=%async_computation.9 | async-start | bytes 139264
  380.4 148.1 %reduce-scatter.10.cloned.1.call-start = ((), (), s32[]{:S(2)}) async-start(), calls=%async_computation.8 | async-start | bytes 1114112
  384.8 278.0 %all-gather.10.cloned.1.call-start = ((), (), s32[]{:S(2)}) async-start(), calls=%async_computation.5 | async-start | bytes 8912896 | tf_op jit(solution)/shard_map/all_gather | solution.py:65
  385.4 288.8 %reduce-scatter.8.cloned.1.call-start = ((), (), s32[]{:S(2)}) async-start(), calls=%async_computation.6 | async-start | bytes 393216 | tf_op jit(solution)/shard_map/reduce_scatter | solution.py:69
  529.6 145.6 %copy-start = (f32[4096]{0:T(1024)S(1)}, f32[4096]{0:T(1024)}, u32[]{:S(2)}) copy-start(f32[4096]{0:T(1024)} %param.13) | copy-start | bytes 49156
  529.6 147.3 %copy-start.1 = (s32[1,16]{1,0:T(1,128)S(1)}, s32[1,16]{1,0:T(1,128)}, u32[]{:S(2)}) copy-start(s32[1,16]{1,0:T(1,128)} %param.17) | copy-start | bytes 196
  668.2 66.9 %all-gather.12.cloned.1.call-start = ((), (), s32[]{:S(2)}) async-start(), calls=%async_computation.7 | async-start | bytes 2162688 | tf_op jit(solution)/shard_map/all_gather | solution.py:72
Sparse Core Ops, SparseCore 0:
  10.1 115.5 all-gather.7
  128.5 193.4 all-gather.5
  380.5 71.6 reduce-scatter.11
  454.5 74.0 reduce-scatter.9
  531.1 131.7 all-gather.9
  668.3 5.8 reduce-scatter.7
  677.4 57.5 all-gather.11
